TPU v7x, 512 devices: a whole 4x4x16 slice. The times are simulated.
512 devices in a mesh: seq: 64 (over z_lo, x, core), dp: 8 (over y, z_hi).
Axes of the slice: x: 4, y: 4, z: 16 (z_hi: 2, z_lo: 8; z = z_hi * 8 + z_lo), core: 2. Of those that a mesh axis runs over, the one named last changes fastest.
Arguments:
- queries: bfloat16 [65536, 2048], P(('dp', 'seq')), parts along dimension 0, may hold values from -20 to 20
- keys: bfloat16 [65536, 2048], P(('dp', 'seq')), parts along dimension 0, may hold values from -20 to 20
- values: bfloat16 [65536, 2048], P(('dp', 'seq')), parts along dimension 0, may hold values from -48 to 48
- cotangent: bfloat16 [65536, 2048], P(('dp', 'seq')), parts along dimension 0, may hold values from -24 to 24
- documents: int32 [65536], P(('dp', 'seq')), parts along dimension 0, may hold values from 0 to 7, never falling along the last dimension, each value on 1 to 6144 neighbouring positions
- global_offsets: int32 [1024], P(('dp', 'seq')), parts along dimension 0, may hold values from 0 to 127
Outputs:
- attended: bfloat16 [65536, 2048], P(('dp', 'seq')), parts along dimension 0
- query_grad: bfloat16 [65536, 2048], P(('dp', 'seq')), parts along dimension 0
- key_grad: bfloat16 [65536, 2048], P(('dp', 'seq')), parts along dimension 0
- value_grad: bfloat16 [65536, 2048], P(('dp', 'seq')), parts along dimension 0
There are 8 independent parts, one for each index of `dp`. A program takes and returns all parts, laid end to end along the dimension named above; each array names one. Nothing has to cross between parts.
All inputs are finite; a program needn't handle non-finite values.
Results may differ from a plain program's by a relative error of at most 0.023.
Values may be sent and summed in bfloat16 or wider, within the bound.
No kernel may reach another device: no remote copies, remote signals or barrier semaphores. Data moves between devices by JAX's collectives and lax.ppermute only.
A program may use at most 64 MiB of HBM per device.

v0:
```python
import jax
import jax.numpy as jnp
from jax import lax
from jax.sharding import PartitionSpec as P

HEADS = 16
LEVELS = 2


def from_partner(array, axis, stride):
    return lax.ppermute(array, axis, [(i, i ^ 1 << stride) for i in range(lax.axis_size(axis))])


def local(queries, keys, values, cotangent, documents, global_offsets):
    rows_here, columns = queries.shape
    head_size = columns // HEADS
    temper = head_size ** (-0.5)
    shards = lax.axis_size("seq")
    myself = lax.axis_index("seq")
    log_shards = shards.bit_length() - 1
    level_bits = [step * (log_shards - 2) // (LEVELS - 1) for step in range(LEVELS)]

    def split(array):
        return array.reshape(array.shape[0], HEADS, head_size)

    every_doc = lax.all_gather(documents, "seq", axis=0, tiled=True)
    picked_keys = keys[global_offsets]
    picked_values = values[global_offsets]
    global_keys, global_values = (
        lax.all_gather(picked_keys, "seq", axis=0, tiled=True),
        lax.all_gather(picked_values, "seq", axis=0, tiled=True),
    )
    global_count = global_keys.shape[0]
    per_block = global_offsets.shape[0]
    owners = jnp.arange(global_count, dtype=jnp.int32) // per_block
    distance = owners ^ myself
    nearby = distance == 0
    for level_bit in level_bits:
        nearby = nearby | (distance == 1 << level_bit)
    query_heads = split(queries)
    dout_heads = split(cotangent)
    key_list = [keys]
    value_list = [values]
    mask_list = [documents[:, None] == documents[None, :]]
    for level_bit in level_bits:
        partner_keys, partner_values = from_partner((keys, values), "seq", level_bit)
        partner_docs = lax.dynamic_slice_in_dim(
            every_doc, (myself ^ 1 << level_bit) * rows_here, rows_here
        )
        key_list.append(partner_keys)
        value_list.append(partner_values)
        mask_list.append(documents[:, None] == partner_docs[None, :])
    block_keys = jnp.concatenate(key_list, 0)
    block_values = jnp.concatenate(value_list, 0)
    block_mask = jnp.concatenate(mask_list, 1)
    raw = (
        jnp.einsum(
            "thd,uhd->htu", query_heads, split(block_keys), preferred_element_type=jnp.float32
        )
        * temper
    )
    block_scores = jnp.where(block_mask[None], raw, -jnp.inf)
    global_raw = (
        jnp.einsum(
            "thd,ghd->htg", query_heads, split(global_keys), preferred_element_type=jnp.float32
        )
        * temper
    )
    global_scores = jnp.where(jnp.logical_not(nearby)[None, None, :], global_raw, -jnp.inf)
    highest = jnp.maximum(jnp.max(global_scores, axis=-1), jnp.max(block_scores, axis=-1))
    block_exp = jnp.exp(block_scores - highest[..., None])
    global_exp = jnp.exp(global_scores - highest[..., None])
    totals = jnp.sum(global_exp, axis=-1) + jnp.sum(block_exp, axis=-1)
    probs = block_exp / totals[..., None]
    global_prob = global_exp / totals[..., None]
    probs_b = probs.astype(jnp.bfloat16)
    global_prob_b = global_prob.astype(jnp.bfloat16)
    summed = jnp.einsum(
        "htg,ghd->thd", global_prob_b, split(global_values), preferred_element_type=jnp.float32
    )
    summed = summed + jnp.einsum(
        "htu,uhd->thd", probs_b, split(block_values), preferred_element_type=jnp.float32
    )
    attended = summed.astype(jnp.bfloat16).reshape(rows_here, columns)
    delta = jnp.sum(dout_heads.astype(jnp.float32) * split(attended).astype(jnp.float32), axis=-1).T
    product = jnp.einsum(
        "thd,uhd->htu", dout_heads, split(block_values), preferred_element_type=jnp.float32
    )
    slope = (probs * (product - delta[:, :, None])).astype(jnp.bfloat16)
    query_term = jnp.einsum(
        "htu,uhd->thd", slope, split(block_keys), preferred_element_type=jnp.float32
    )
    key_term = temper * jnp.einsum(
        "htu,thd->uhd", slope, query_heads, preferred_element_type=jnp.float32
    )
    value_term = jnp.einsum("htu,thd->uhd", probs_b, dout_heads, preferred_element_type=jnp.float32)
    query_sum = query_term
    key_sum = key_term[:rows_here]
    value_sum = value_term[:rows_here]
    for level, level_bit in enumerate(level_bits):
        lower = (level + 1) * rows_here
        upper = (level + 2) * rows_here
        back_keys, back_values = from_partner(
            (
                key_term[lower:upper].reshape(rows_here, columns).astype(jnp.bfloat16),
                value_term[lower:upper].reshape(rows_here, columns).astype(jnp.bfloat16),
            ),
            "seq",
            level_bit,
        )
        key_sum = key_sum + split(back_keys).astype(jnp.float32)
        value_sum = value_sum + split(back_values).astype(jnp.float32)
    global_product = jnp.einsum(
        "thd,ghd->htg", dout_heads, split(global_values), preferred_element_type=jnp.float32
    )
    global_slope = (global_prob * (global_product - delta[:, :, None])).astype(jnp.bfloat16)
    query_sum = query_sum + jnp.einsum(
        "htg,ghd->thd", global_slope, split(global_keys), preferred_element_type=jnp.float32
    )
    key_part = temper * jnp.einsum(
        "htg,thd->ghd", global_slope, query_heads, preferred_element_type=jnp.float32
    )
    value_part = jnp.einsum(
        "htg,thd->ghd", global_prob_b, dout_heads, preferred_element_type=jnp.float32
    )
    owned = lax.psum_scatter(
        jnp.concatenate(
            [
                key_part.reshape(per_block * lax.axis_size("seq"), columns),
                value_part.reshape(per_block * lax.axis_size("seq"), columns),
            ],
            1,
        ),
        "seq",
        scatter_dimension=0,
        tiled=True,
    )
    placement = (jnp.arange(rows_here, dtype=jnp.int32)[:, None] == global_offsets[None, :]).astype(
        jnp.float32
    )
    spread_rows = jnp.dot(
        placement, owned, precision=lax.Precision.HIGHEST, preferred_element_type=jnp.float32
    )
    key_grad = (key_sum.reshape(rows_here, columns) + spread_rows[:, :columns]).astype(jnp.bfloat16)
    value_grad = (value_sum.reshape(rows_here, columns) + spread_rows[:, columns:]).astype(
        jnp.bfloat16
    )
    query_grad = (temper * query_sum).reshape(rows_here, columns).astype(jnp.bfloat16)
    return (attended, query_grad, key_grad, value_grad)


def solution(mesh):
    in_specs = (
        P(("dp", "seq"), None),
        P(("dp", "seq"), None),
        P(("dp", "seq"), None),
        P(("dp", "seq"), None),
        P(("dp", "seq")),
        P(("dp", "seq")),
    )
    out_specs = (
        P(("dp", "seq"), None),
        P(("dp", "seq"), None),
        P(("dp", "seq"), None),
        P(("dp", "seq"), None),
    )
    return jax.shard_map(local, mesh=mesh, in_specs=in_specs, out_specs=out_specs, check_vma=False)
```

profile of v0, /device:TPU:1, one launch (start us, length us, event | category | flops | bytes accessed | tf_op | source)
XLA Modules:
  0.0 1265.3 jit_solution(16097213967234120717)
XLA Ops:
  7.2 1.4 copy.77
  8.6 5.7 collective-permute-start.1
  14.3 5.0 collective-permute-start
  19.3 4.5 collective-permute-start.3
  23.8 2.2 collective-permute-start.2
  26.7 1.7 gather_fusion
  28.4 1.7 gather_fusion.1
  30.1 124.5 %all-gather.2 = bf16[64,2,2048]{2,1,0:T(2,128)(2,1)S(1)} all-gather(bf16[1,2,2048]{2,1,0:T(2,128)(2,1)S(1)} %bitcast.117), channel_id=2, replica_groups=mesh['seq'=64,'dp'=8] {'seq'}, dimensions={0}, use_global_device_ids=true | all-gather | bytes 532480 | tf_op jit(solution)/shard_map/all_gather | solution.py:31
  154.6 113.8 %all-gather.3 = bf16[64,2,2048]{2,1,0:T(2,128)(2,1)S(1)} all-gather(bf16[1,2,2048]{2,1,0:T(2,128)(2,1)S(1)} %bitcast.116), channel_id=3, replica_groups=mesh['seq'=64,'dp'=8] {'seq'}, dimensions={0}, use_global_device_ids=true | all-gather | bytes 532480 | tf_op jit(solution)/shard_map/all_gather | solution.py:30
  268.4 114.1 %all-gather.4 = s32[64,1,128]{2,1,0:T(1,128)S(1)} all-gather(s32[1,1,128]{2,1,0:T(1,128)} %bitcast.118), channel_id=1, replica_groups=mesh['seq'=64,'dp'=8] {'seq'}, dimensions={0}, use_global_device_ids=true | all-gather | bytes 33280 | tf_op jit(solution)/shard_map/all_gather | solution.py:26
  382.6 0.8 broadcast_compare_fusion.2
  383.5 2.0 copy.84
  385.5 1.1 reshape.104
  387.7 1.3 dynamic-slice
  390.1 0.8 copy-done.12
  390.9 1.4 pad_maximum_fusion.1
  393.3 1.4 copy-done
  395.4 2.5 pad_maximum_fusion.2
  398.0 2.7 copy.82
  400.7 2.0 fusion.23
  403.5 2.1 multiply_reduce_fusion
  406.0 2.6 fusion
  408.6 3.2 fusion.39
  411.8 1.5 fusion.30
  413.2 2.0 copy.108
  415.3 1.5 fusion.6
  416.7 2.6 copy.103
  419.3 3.0 pad_maximum_fusion
  422.4 2.4 fusion.35
  424.8 1.9 collective-permute-start.7
  426.7 2.1 collective-permute-start.6
  428.8 2.3 fusion.40
  431.2 1.0 copy.97
  432.2 4.7 collective-permute-start.5
  437.0 1.0 copy.95
  438.0 2.2 collective-permute-start.4
  440.2 1.3 fusion.41
  441.6 2.0 fusion.12
  443.6 1.0 copy.109
  444.6 4.2 collective-permute-done.7
  448.8 1.7 fusion.16
  450.9 9.7 collective-permute-done.5
  460.8 1.2 copy.96
  462.0 2.4 fusion.18
  464.4 1.6 copy.99
  466.3 787.9 %all-reduce.3.cloned.1.call-done = f32[128,4096]{0,1:T(8,128)} async-done(((f32[128,4096]{0,1:T(8,128)}), f32[128,4096]{0,1:T(8,128)}) %all-reduce.3.cloned.1.call-update) | async-done | bytes 2097168
  1254.2 3.0 fusion.4
  1257.2 1.2 fusion.15
  (53 shorter events, 6.1 us)
Async XLA Ops:
  7.2 380.3 %copy-start.8 = (bf16[128,2048]{1,0:T(8,128)(2,1)S(1)}, bf16[128,2048]{1,0:T(8,128)(2,1)}, u32[]{:S(2)}) copy-start(bf16[128,2048]{1,0:T(8,128)(2,1)} %param.6) | copy-start | bytes 1572868
  7.2 1247.0 %all-reduce.3.cloned.1.call-start = ((), (), s32[]{:S(2)}) async-start(), calls=%async_computation | async-start | bytes 4194304
  8.6 381.5 %collective-permute-start.1 = (bf16[128,2048]{0,1:T(8,128)(2,1)S(1)}, bf16[128,2048]{0,1:T(8,128)(2,1)S(1)}, u32[]{:S(2)}, u32[]{:S(2)}) collective-permute-start(bf16[128,2048]{0,1:T(8,128)(2,1)S(1)} %copy.77), channel_id=1, source_target_pairs={{0,128},{8,136},{16,144},{24,152},{32,160},{40,168},{48,176},{56,1... | collective-permute-start | bytes 1572872 | tf_op jit(solution)/shard_map/ppermute | solution.py:11
  14.3 376.6 %collective-permute-start = (bf16[128,2048]{0,1:T(8,128)(2,1)S(1)}, bf16[128,2048]{0,1:T(8,128)(2,1)}, u32[]{:S(2)}, u32[]{:S(2)}) collective-permute-start(bf16[128,2048]{0,1:T(8,128)(2,1)S(1)} %copy.77), channel_id=1, source_target_pairs={{0,8},{8,0},{16,24},{24,16},{32,40},{40,32},{48,56},{56,48},{64,72... | collective-permute-start | bytes 1572872 | tf_op jit(solution)/shard_map/ppermute | solution.py:11
  19.3 376.2 %collective-permute-start.3 = (bf16[128,2048]{1,0:T(8,128)(2,1)}, bf16[128,2048]{1,0:T(8,128)(2,1)}, u32[]{:S(2)}, u32[]{:S(2)}) collective-permute-start(bf16[128,2048]{1,0:T(8,128)(2,1)} %param.8), channel_id=1, source_target_pairs={{0,128},{8,136},{16,144},{24,152},{32,160},{40,168},{48,176},{56,1... | collective-permute-start | bytes 1572872 | tf_op jit(solution)/shard_map/ppermute | solution.py:11
  23.8 371.6 %collective-permute-start.2 = (bf16[128,2048]{1,0:T(8,128)(2,1)}, bf16[128,2048]{1,0:T(8,128)(2,1)}, u32[]{:S(2)}, u32[]{:S(2)}) collective-permute-start(bf16[128,2048]{1,0:T(8,128)(2,1)} %param.8), channel_id=1, source_target_pairs={{0,8},{8,0},{16,24},{24,16},{32,40},{40,32},{48,56},{56,48},{64,72... | collective-permute-start | bytes 1572872 | tf_op jit(solution)/shard_map/ppermute | solution.py:11
  390.1 3.1 copy-start.3
  390.1 0.8 copy-start.12
  393.1 1.7 copy-start
  393.1 2.3 copy-start.7
  398.0 4.7 copy-start.9
  400.6 2.4 copy-start.1
  400.6 2.8 copy-start.6
  403.5 2.1 copy-start.4
  403.5 2.1 copy-start.10
  403.5 2.1 copy-start.11
  406.0 9.3 copy-start.5
  422.4 6.4 copy-start.2
  424.8 24.0 %collective-permute-start.7 = (bf16[128,2048]{0,1:T(8,128)(2,1)}, bf16[128,2048]{0,1:T(8,128)(2,1)}, u32[]{:S(2)}, u32[]{:S(2)}) collective-permute-start(bf16[128,2048]{0,1:T(8,128)(2,1)} %bitcast.29), channel_id=1, source_target_pairs={{0,128},{8,136},{16,144},{24,152},{32,160},{40,168},{48,176},{56,1... | collective-permute-start | bytes 1572872 | tf_op jit(solution)/shard_map/ppermute | solution.py:11
  426.7 22.1 %collective-permute-start.6 = (bf16[128,2048]{0,1:T(8,128)(2,1)}, bf16[128,2048]{0,1:T(8,128)(2,1)}, u32[]{:S(2)}, u32[]{:S(2)}) collective-permute-start(bf16[128,2048]{0,1:T(8,128)(2,1)} %bitcast.27), channel_id=1, source_target_pairs={{0,8},{8,0},{16,24},{24,16},{32,40},{40,32},{48,56},{56,48},{64,72... | collective-permute-start | bytes 1572872 | tf_op jit(solution)/shard_map/ppermute | solution.py:11
  432.2 28.3 %collective-permute-start.5 = (bf16[128,2048]{0,1:T(8,128)(2,1)}, bf16[128,2048]{0,1:T(8,128)(2,1)S(1)}, u32[]{:S(2)}, u32[]{:S(2)}) collective-permute-start(bf16[128,2048]{0,1:T(8,128)(2,1)} %bitcast.112), channel_id=1, source_target_pairs={{0,128},{8,136},{16,144},{24,152},{32,160},{40,168},{48,176},{56,1... | collective-permute-start | bytes 1572872 | tf_op jit(solution)/shard_map/ppermute | solution.py:11
  438.0 22.8 %collective-permute-start.4 = (bf16[128,2048]{0,1:T(8,128)(2,1)}, bf16[128,2048]{0,1:T(8,128)(2,1)}, u32[]{:S(2)}, u32[]{:S(2)}) collective-permute-start(bf16[128,2048]{0,1:T(8,128)(2,1)} %bitcast.113), channel_id=1, source_target_pairs={{0,8},{8,0},{16,24},{24,16},{32,40},{40,32},{48,56},{56,48},{64,72... | collective-permute-start | bytes 1572872 | tf_op jit(solution)/shard_map/ppermute | solution.py:11
  464.4 789.8 %copy-start.13 = (s32[2]{0:T(128)S(1)}, s32[2]{0:T(128)}, u32[]{:S(2)}) copy-start(s32[2]{0:T(128)} %param.11) | copy-start | bytes 28
Sparse Core Ops, SparseCore 0:
  422.5 831.6 all-reduce.2
where the time goes:
time: 1270 us
  waiting for transfers between devices  802 us (63%)
  blocking collectives  352 us (28%)
  local copies, waits for them, and re-layouts  30 us (2%)
  starting transfers between devices  28.4 us (2%)
  matrix products  23 us (2%)
  between operations  15.1 us (1%)
  other arithmetic  14.6 us (1%)
    unnamed x2, waiting for transfers between devices  788 us
    all_gather x1, blocking collectives, local(): lax.all_gather(picked_values, 'seq', axis=0, tiled=True)  125 us
    all_gather x1, blocking collectives, local(): every_doc = lax.all_gather(documents, 'seq', axis=0, tiled=True)  114 us
    all_gather x1, blocking collectives, local(): lax.all_gather(picked_keys, 'seq', axis=0, tiled=True)  114 us
    ppermute x8, starting transfers between devices, from_partner(): lax.ppermute(array, axis, [(i, i ^ 1 << stride) for i in range(lax.axis_s...  28.4 us
  transfers between devices with their start and end apart: 9, of which 3 were waited for; matrix products, arithmetic and copies ran while one was open for 3% of the time, Pallas kernels for 0%

commit v1 on v0

--- a/solution.py
+++ b/solution.py
@@ -28,7 +28,9 @@
     picked_values = values[global_offsets]
     global_keys, global_values = (
         lax.all_gather(picked_keys, "seq", axis=0, tiled=True),
-        lax.all_gather(picked_values, "seq", axis=0, tiled=True),
+        jnp.concatenate(
+            lax.all_to_all(jnp.stack([picked_values] * lax.axis_size("seq")), "seq", 0, 0), axis=0
+        ),
     )
     global_count = global_keys.shape[0]
     per_block = global_offsets.shape[0]

time: 1270 us -> 1180 us (0.929)
  blocking collectives: 352 us -> 237 us
    all_gather x1 -> x0, blocking collectives: 125 us -> none  [local(): lax.all_gather(picked_values, 'seq', axis=0, tiled=True)]
    unnamed x2, waiting for transfers between devices: 788 us -> 802 us
  transfers between devices with their start and end apart: 9 -> 10, of which waited for: 3 -> 3; matrix products, arithmetic and copies ran while one was open for 3% -> 4% of each run, Pallas kernels for 0% -> 0%
where the time goes in v1:
time: 1180 us
  waiting for transfers between devices  812 us (69%)
  blocking collectives  237 us (20%)
  starting transfers between devices  37.2 us (3%)
  local copies, waits for them, and re-layouts  32.9 us (3%)
  matrix products  27.8 us (2%)
  other arithmetic  15.1 us (1%)
  between operations  15.1 us (1%)
    unnamed x2, waiting for transfers between devices  802 us
    all_gather x1, blocking collectives, local(): lax.all_gather(picked_keys, 'seq', axis=0, tiled=True)  125 us
    all_gather x1, blocking collectives, local(): every_doc = lax.all_gather(documents, 'seq', axis=0, tiled=True)  112 us
    ppermute x8, starting transfers between devices, from_partner(): lax.ppermute(array, axis, [(i, i ^ 1 << stride) for i in range(lax.axis_s...  26.7 us
  transfers between devices with their start and end apart: 10, of which 3 were waited for; matrix products, arithmetic and copies ran while one was open for 4% of the time, Pallas kernels for 0%

profile of v1, /device:TPU:1, one launch (start us, length us, event | category | flops | bytes accessed | tf_op | source)
XLA Modules:
  0.0 1177.3 jit_solution(1356985948944871817)
XLA Ops:
  7.2 1.4 copy.77
  8.6 5.7 collective-permute-start.1
  14.3 5.0 collective-permute-start
  19.3 4.5 collective-permute-start.3
  23.8 2.2 collective-permute-start.2
  26.7 1.7 gather_fusion
  28.4 1.1 stack.2
  29.5 10.4 all-to-all-start
  39.9 1.7 gather_fusion.1
  41.6 124.8 %all-gather.1 = bf16[64,2,2048]{2,1,0:T(2,128)(2,1)S(1)} all-gather(bf16[1,2,2048]{2,1,0:T(2,128)(2,1)S(1)} %bitcast.115), channel_id=2, replica_groups=mesh['seq'=64,'dp'=8] {'seq'}, dimensions={0}, use_global_device_ids=true | all-gather | bytes 532480 | tf_op jit(solution)/shard_map/all_gather | solution.py:30
  166.4 112.5 %all-gather.2 = s32[64,1,128]{2,1,0:T(1,128)S(1)} all-gather(s32[1,1,128]{2,1,0:T(1,128)S(1)} %bitcast.116), channel_id=1, replica_groups=mesh['seq'=64,'dp'=8] {'seq'}, dimensions={0}, use_global_device_ids=true | all-gather | bytes 33280 | tf_op jit(solution)/shard_map/all_gather | solution.py:26
  281.2 1.3 dynamic-slice
  284.4 1.6 pad_maximum_fusion.1
  288.2 2.8 fusion.39
  291.0 1.3 fusion.35
  292.2 1.9 collective-permute-start.7
  294.2 2.3 collective-permute-start.6
  296.5 2.5 pad_maximum_fusion.2
  299.0 2.6 copy.82
  301.6 2.8 fusion.30
  304.5 4.2 collective-permute-done.7
  308.7 2.7 fusion.16
  311.3 2.5 copy.124
  313.8 1.1 reshape_reshape.4
  315.0 2.0 fusion.23
  317.4 3.5 multiply_reduce_fusion
  320.9 2.0 copy.108
  322.9 1.8 fusion.13
  325.5 1.5 fusion.6
  327.0 2.6 copy.103
  329.6 3.0 pad_maximum_fusion
  332.6 3.7 fusion
  336.3 2.2 fusion.40
  338.7 1.0 copy.97
  339.7 2.2 collective-permute-start.5
  341.9 1.0 copy.95
  342.9 2.9 collective-permute-start.4
  345.8 1.3 fusion.41
  347.2 2.0 fusion.12
  349.2 1.0 copy.109
  350.2 5.3 collective-permute-done.5
  355.8 1.2 copy.96
  357.0 2.4 fusion.18
  359.5 2.6 copy.99
  362.1 1.6 copy.105
  363.7 802.5 %all-reduce.3.cloned.1.call-done = f32[128,4096]{0,1:T(8,128)} async-done(((f32[128,4096]{0,1:T(8,128)}), f32[128,4096]{0,1:T(8,128)}) %all-reduce.3.cloned.1.call-update) | async-done | bytes 2097168
  1166.2 3.0 fusion.4
  1169.3 1.2 fusion.15
  (57 shorter events, 8.0 us)
Async XLA Ops:
  7.2 159.3 %copy-start.13 = (s32[128]{0:T(128)S(1)}, s32[128]{0:T(128)}, u32[]{:S(2)}) copy-start(s32[128]{0:T(128)} %param.10) | copy-start | bytes 1540
  7.2 271.9 %copy-start.8 = (bf16[128,2048]{1,0:T(8,128)(2,1)S(1)}, bf16[128,2048]{1,0:T(8,128)(2,1)}, u32[]{:S(2)}) copy-start(bf16[128,2048]{1,0:T(8,128)(2,1)} %param.9) | copy-start | bytes 1572868
  7.2 273.7 %copy-start.9 = (bf16[128,2048]{1,0:T(8,128)(2,1)S(1)}, bf16[128,2048]{1,0:T(8,128)(2,1)}, u32[]{:S(2)}) copy-start(bf16[128,2048]{1,0:T(8,128)(2,1)} %param.6) | copy-start | bytes 1572868
  8.6 272.6 %copy-start.5 = (bf16[128,2048]{0,1:T(8,128)(2,1)}, bf16[128,2048]{0,1:T(8,128)(2,1)S(1)}, u32[]{:S(2)}) copy-start(bf16[128,2048]{0,1:T(8,128)(2,1)S(1)} %copy.77) | copy-start | bytes 1572868
  8.6 274.9 %collective-permute-start.1 = (bf16[128,2048]{0,1:T(8,128)(2,1)S(1)}, bf16[128,2048]{0,1:T(8,128)(2,1)S(1)}, u32[]{:S(2)}, u32[]{:S(2)}) collective-permute-start(bf16[128,2048]{0,1:T(8,128)(2,1)S(1)} %copy.77), channel_id=1, source_target_pairs={{0,128},{8,136},{16,144},{24,152},{32,160},{40,168},{48,176},{56,1... | collective-permute-start | bytes 1572872 | tf_op jit(solution)/shard_map/ppermute | solution.py:11
  14.3 270.1 %collective-permute-start = (bf16[128,2048]{0,1:T(8,128)(2,1)S(1)}, bf16[128,2048]{0,1:T(8,128)(2,1)}, u32[]{:S(2)}, u32[]{:S(2)}) collective-permute-start(bf16[128,2048]{0,1:T(8,128)(2,1)S(1)} %copy.77), channel_id=1, source_target_pairs={{0,8},{8,0},{16,24},{24,16},{32,40},{40,32},{48,56},{56,48},{64,72... | collective-permute-start | bytes 1572872 | tf_op jit(solution)/shard_map/ppermute | solution.py:11
  19.3 277.1 %collective-permute-start.3 = (bf16[128,2048]{1,0:T(8,128)(2,1)}, bf16[128,2048]{1,0:T(8,128)(2,1)}, u32[]{:S(2)}, u32[]{:S(2)}) collective-permute-start(bf16[128,2048]{1,0:T(8,128)(2,1)} %param.8), channel_id=1, source_target_pairs={{0,128},{8,136},{16,144},{24,152},{32,160},{40,168},{48,176},{56,1... | collective-permute-start | bytes 1572872 | tf_op jit(solution)/shard_map/ppermute | solution.py:11
  23.8 272.6 %collective-permute-start.2 = (bf16[128,2048]{1,0:T(8,128)(2,1)}, bf16[128,2048]{1,0:T(8,128)(2,1)}, u32[]{:S(2)}, u32[]{:S(2)}) collective-permute-start(bf16[128,2048]{1,0:T(8,128)(2,1)} %param.8), channel_id=1, source_target_pairs={{0,8},{8,0},{16,24},{24,16},{32,40},{40,32},{48,56},{56,48},{64,72... | collective-permute-start | bytes 1572872 | tf_op jit(solution)/shard_map/ppermute | solution.py:11
  29.5 284.4 %all-to-all-start = ((bf16[64,2,2048]{2,1,0:T(2,128)(2,1)}), bf16[64,2,2048]{2,1,0:T(2,128)(2,1)S(1)}, u32[]{:S(2)}, u32[]{:S(2)}) async-start(bf16[64,2,2048]{2,1,0:T(2,128)(2,1)} %stack.2), calls=%async_computation | async-start | bytes 1048576 | tf_op jit(solution)/shard_map/all_to_all | solution.py:32
  39.9 1126.3 %all-reduce.3.cloned.1.call-start = ((), (), s32[]{:S(2)}) async-start(), calls=%async_computation.1 | async-start | bytes 4194304
  283.5 3.3 copy-start.4
  283.6 0.8 copy-start.12
  286.8 4.2 copy-start
  286.8 1.4 copy-start.10
  288.2 8.2 copy-start.7
  292.2 16.4 %collective-permute-start.7 = (bf16[128,2048]{0,1:T(8,128)(2,1)}, bf16[128,2048]{0,1:T(8,128)(2,1)}, u32[]{:S(2)}, u32[]{:S(2)}) collective-permute-start(bf16[128,2048]{0,1:T(8,128)(2,1)} %bitcast.28), channel_id=1, source_target_pairs={{0,128},{8,136},{16,144},{24,152},{32,160},{40,168},{48,176},{56,1... | collective-permute-start | bytes 1572872 | tf_op jit(solution)/shard_map/ppermute | solution.py:11
  294.2 14.5 %collective-permute-start.6 = (bf16[128,2048]{0,1:T(8,128)(2,1)}, bf16[128,2048]{0,1:T(8,128)(2,1)}, u32[]{:S(2)}, u32[]{:S(2)}) collective-permute-start(bf16[128,2048]{0,1:T(8,128)(2,1)} %bitcast.26), channel_id=1, source_target_pairs={{0,8},{8,0},{16,24},{24,16},{32,40},{40,32},{48,56},{56,48},{64,72... | collective-permute-start | bytes 1572872 | tf_op jit(solution)/shard_map/ppermute | solution.py:11
  315.0 2.4 copy-start.1
  315.0 2.5 copy-start.11
  324.7 0.8 copy-start.6
  336.3 2.3 copy-start.2
  339.7 15.9 %collective-permute-start.5 = (bf16[128,2048]{0,1:T(8,128)(2,1)}, bf16[128,2048]{0,1:T(8,128)(2,1)S(1)}, u32[]{:S(2)}, u32[]{:S(2)}) collective-permute-start(bf16[128,2048]{0,1:T(8,128)(2,1)} %bitcast.111), channel_id=1, source_target_pairs={{0,128},{8,136},{16,144},{24,152},{32,160},{40,168},{48,176},{56,1... | collective-permute-start | bytes 1572872 | tf_op jit(solution)/shard_map/ppermute | solution.py:11
  342.9 12.9 %collective-permute-start.4 = (bf16[128,2048]{0,1:T(8,128)(2,1)}, bf16[128,2048]{0,1:T(8,128)(2,1)}, u32[]{:S(2)}, u32[]{:S(2)}) collective-permute-start(bf16[128,2048]{0,1:T(8,128)(2,1)} %bitcast.112), channel_id=1, source_target_pairs={{0,8},{8,0},{16,24},{24,16},{32,40},{40,32},{48,56},{56,48},{64,72... | collective-permute-start | bytes 1572872 | tf_op jit(solution)/shard_map/ppermute | solution.py:11
  359.5 806.7 %copy-start.14 = (s32[2]{0:T(128)S(1)}, s32[2]{0:T(128)}, u32[]{:S(2)}) copy-start(s32[2]{0:T(128)} %param.11) | copy-start | bytes 28
  362.1 807.2 %copy-start.3 = (f32[128,2048]{1,0:T(8,128)S(1)}, f32[128,2048]{1,0:T(8,128)}, u32[]{:S(2)}) copy-start(f32[128,2048]{1,0:T(8,128)} %copy.124) | copy-start | bytes 3145732
Sparse Core Ops, SparseCore 0:
  332.7 833.4 all-reduce.2
